TPU v7x, 256 devices: a whole 4x4x8 slice. The times are simulated.
256 devices in a mesh: dp: 16 (over x, y_lo, core), expert: 16 (over z, y_hi).
Axes of the slice: x: 4, y: 4 (y_hi: 2, y_lo: 2; y = y_hi * 2 + y_lo), z: 8, core: 2. Of those that a mesh axis runs over, the one named last changes fastest.
Arguments:
- tokens: bfloat16 [32768, 2048], P(('dp', 'expert')), may hold values from -6 to 6
- gain: float32 [2048], replicated, may hold values from 0.1 to 1.9
- expert_ids: int32 [32768, 8], P(('dp', 'expert')), may hold values from 0 to 15, all different within a row; in each aligned block of 128 rows (0 to 127, 128 to 255, ...) at most 96 rows name the same one
- gate_values: float32 [32768, 8], P(('dp', 'expert')), may hold values from 0.02 to 0.25
- w_gate: bfloat16 [16, 2048, 768], P('expert'), may hold values from -0.125 to 0.125
- w_up: bfloat16 [16, 2048, 768], P('expert'), may hold values from -0.125 to 0.125
- w_down: bfloat16 [16, 768, 2048], P('expert'), may hold values from -0.21875 to 0.21875
Outputs:
- mixed: bfloat16 [32768, 2048], P(('dp', 'expert'))
Inputs may be any that keep to these rules, and one draw needn't show every extreme that they name: `expert_ids`: each row names 8 different experts. In the rows of one device no expert is named by more than 96 rows, and in every draw some expert is named by exactly 96 rows of some device.
All inputs are finite; a program needn't handle non-finite values.
Results may differ from a plain program's by a relative error of at most 0.018.
Values may be sent and summed in bfloat16 or wider, within the bound.
No kernel may reach another device: no remote copies, remote signals or barrier semaphores. Data moves between devices by JAX's collectives and lax.ppermute only.
A program may use at most 128 MiB of HBM per device.

v0:
```python
import jax
import jax.numpy as jnp
from jax import lax
from jax.sharding import PartitionSpec as P

eps_value = 1e-06


def passed_along(block, axis, distance):
    devices = range(lax.axis_size(axis))
    route = [((i - distance) % len(devices), i) for i in devices]
    return lax.ppermute(block, axis, route)


def normalize(tokens, gain):
    values = tokens.astype(jnp.float32)
    meansq = jnp.mean(values * values, axis=-1, keepdims=True)
    return (values * lax.rsqrt(meansq + eps_value) * gain).astype(jnp.bfloat16)


def gate_dense(expert_ids, gate_values, number):
    labels = jnp.arange(number, dtype=jnp.int32)
    hits = (expert_ids[..., None] == labels).astype(jnp.float32)
    return jnp.sum(hits * gate_values[..., None], axis=-2)


def dispatch_table(column, capacity):
    matched = (column > 0).astype(jnp.float32)
    slots = jnp.cumsum(matched, axis=-1) - 1.0
    places = jnp.arange(capacity).astype(jnp.float32)
    chosen = (slots[..., None, :] == places[:, None]) & (matched[..., None, :] > 0)
    return chosen.astype(jnp.bfloat16)


def expert_mlp(slot_rows, gate_matrix, up_matrix, down_matrix):
    gated = jnp.dot(slot_rows, gate_matrix, preferred_element_type=jnp.float32)
    upward = jnp.dot(slot_rows, up_matrix, preferred_element_type=jnp.float32)
    hidden = (jax.nn.silu(gated) * upward).astype(jnp.bfloat16)
    return jnp.dot(hidden, down_matrix, preferred_element_type=jnp.float32).astype(jnp.bfloat16)


def place_block(buffer, table, carried, source):
    picked = lax.dynamic_index_in_dim(table, source, 0, keepdims=False)
    slot_rows = jnp.dot(picked, carried, preferred_element_type=jnp.float32).astype(jnp.bfloat16)
    return lax.dynamic_update_index_in_dim(buffer, slot_rows, source, 0)


def local(tokens, gain, expert_ids, gate_values, w_gate, w_up, w_down):
    group = lax.axis_size("expert")
    position = lax.axis_index("expert")
    local_rows = tokens.shape[0]
    width = tokens.shape[1]
    chosen_count = expert_ids.shape[1]
    capacity = local_rows * chosen_count // group * 3 // 2
    gate_matrix = w_gate[0]
    up_matrix = w_up[0]
    down_matrix = w_down[0]
    normed = normalize(tokens, gain)
    dense = gate_dense(expert_ids, gate_values, group)
    gathered = lax.all_gather(dense, "expert", axis=0, tiled=True)
    column = lax.dynamic_slice_in_dim(gathered, position, 1, 1).reshape(group, local_rows)
    table = dispatch_table(column, capacity)
    buffer = jnp.zeros((group, capacity, width), jnp.bfloat16)
    buffer = place_block(buffer, table, normed, position)

    def forward_turn(offset, state):
        current, carried = state
        carried = passed_along(carried, "expert", 1)
        source = (position - offset) % group
        return (place_block(current, table, carried, source), carried)

    buffer, carried = lax.fori_loop(1, group, forward_turn, (buffer, normed))
    outputs = expert_mlp(
        buffer.reshape(group * capacity, width), gate_matrix, up_matrix, down_matrix
    )
    outputs = outputs.reshape(group, capacity, width)
    spanned = local_rows * lax.axis_size("expert") // local_rows
    back = jnp.einsum("bct,bcd->btd", table, outputs, preferred_element_type=jnp.float32)
    return lax.psum_scatter(
        (back * column[:, :, None]).reshape(spanned * local_rows, width).astype(jnp.bfloat16),
        "expert",
        scatter_dimension=0,
        tiled=True,
    )


def solution(mesh):
    return jax.shard_map(
        local,
        mesh=mesh,
        in_specs=(
            P(("dp", "expert"), None),
            P(),
            P(("dp", "expert"), None),
            P(("dp", "expert"), None),
            P("expert", None, None),
            P("expert", None, None),
            P("expert", None, None),
        ),
        out_specs=P(("dp", "expert"), None),
        check_vma=False,
    )
```

profile of v0, /device:TPU:2, one launch (start us, length us, event | category | flops | bytes accessed | tf_op | source)
XLA Modules:
  0.0 603.0 jit_solution(9800306333503433712)
XLA Ops:
  9.3 44.7 %all_gather.3 = f32[2048,16]{0,1:T(8,128)S(1)} all-gather(f32[128,16]{0,1:T(8,128)S(1)} %select_reduce_fusion), channel_id=1, replica_groups=mesh['dp'=16,'expert'=16] {'expert'}, dimensions={0}, use_global_device_ids=true | all-gather | bytes 139264 | tf_op jit(solution)/shard_map/all_gather | solution.py:60
  58.2 2.6 copy-done.1
  60.8 287.0 %while.17 = (s32[]{:T(128)}, bf16[16,96,2048]{2,1,0:T(8,128)(2,1)}, bf16[128,2048]{1,0:T(8,128)(2,1)}, s32[]{:T(128)}, bf16[16,96,128]{2,1,0:T(8,128)(2,1)S(1)},...) while((s32[]{:T(128)}, bf16[16,96,2048]{2,1,0:T(8,128)(2,1)}, bf16[128,2048]{1,0:T(8,128)(2,1)}, s32[]{:T(128)}, ...), condition=%wide.region_4.5_spmd, body=%wide.region_3.4_spmd.sunk | while | flops 50528272 | bytes 4089120 | solution.py:72
  60.8 13.1 %collective-permute-done = bf16[128,2048]{1,0:T(8,128)(2,1)} collective-permute-done((bf16[128,2048]{1,0:T(8,128)(2,1)}, bf16[128,2048]{1,0:T(8,128)(2,1)}, u32[]{:S(2)}, u32[]{:S(2)}) %collective-permute-start) | collective-permute-done | bytes 524320 | tf_op jit(solution)/shard_map/while/body/eval_jaxpr/ppermute | solution.py:12
  77.8 13.1 %collective-permute-done = bf16[128,2048]{1,0:T(8,128)(2,1)} collective-permute-done((bf16[128,2048]{1,0:T(8,128)(2,1)}, bf16[128,2048]{1,0:T(8,128)(2,1)}, u32[]{:S(2)}, u32[]{:S(2)}) %collective-permute-start) | collective-permute-done | bytes 524320 | tf_op jit(solution)/shard_map/while/body/eval_jaxpr/ppermute | solution.py:12
  92.8 2.1 fusion.29
  94.9 13.5 %collective-permute-done = bf16[128,2048]{1,0:T(8,128)(2,1)} collective-permute-done((bf16[128,2048]{1,0:T(8,128)(2,1)}, bf16[128,2048]{1,0:T(8,128)(2,1)}, u32[]{:S(2)}, u32[]{:S(2)}) %collective-permute-start) | collective-permute-done | bytes 524320 | tf_op jit(solution)/shard_map/while/body/eval_jaxpr/ppermute | solution.py:12
  112.4 14.6 %collective-permute-done = bf16[128,2048]{1,0:T(8,128)(2,1)} collective-permute-done((bf16[128,2048]{1,0:T(8,128)(2,1)}, bf16[128,2048]{1,0:T(8,128)(2,1)}, u32[]{:S(2)}, u32[]{:S(2)}) %collective-permute-start) | collective-permute-done | bytes 524320 | tf_op jit(solution)/shard_map/while/body/eval_jaxpr/ppermute | solution.py:12
  131.0 15.8 %collective-permute-done = bf16[128,2048]{1,0:T(8,128)(2,1)} collective-permute-done((bf16[128,2048]{1,0:T(8,128)(2,1)}, bf16[128,2048]{1,0:T(8,128)(2,1)}, u32[]{:S(2)}, u32[]{:S(2)}) %collective-permute-start) | collective-permute-done | bytes 524320 | tf_op jit(solution)/shard_map/while/body/eval_jaxpr/ppermute | solution.py:12
  150.7 16.9 %collective-permute-done = bf16[128,2048]{1,0:T(8,128)(2,1)} collective-permute-done((bf16[128,2048]{1,0:T(8,128)(2,1)}, bf16[128,2048]{1,0:T(8,128)(2,1)}, u32[]{:S(2)}, u32[]{:S(2)}) %collective-permute-start) | collective-permute-done | bytes 524320 | tf_op jit(solution)/shard_map/while/body/eval_jaxpr/ppermute | solution.py:12
  171.6 18.1 %collective-permute-done = bf16[128,2048]{1,0:T(8,128)(2,1)} collective-permute-done((bf16[128,2048]{1,0:T(8,128)(2,1)}, bf16[128,2048]{1,0:T(8,128)(2,1)}, u32[]{:S(2)}, u32[]{:S(2)}) %collective-permute-start) | collective-permute-done | bytes 524320 | tf_op jit(solution)/shard_map/while/body/eval_jaxpr/ppermute | solution.py:12
  193.6 18.2 %collective-permute-done = bf16[128,2048]{1,0:T(8,128)(2,1)} collective-permute-done((bf16[128,2048]{1,0:T(8,128)(2,1)}, bf16[128,2048]{1,0:T(8,128)(2,1)}, u32[]{:S(2)}, u32[]{:S(2)}) %collective-permute-start) | collective-permute-done | bytes 524320 | tf_op jit(solution)/shard_map/while/body/eval_jaxpr/ppermute | solution.py:12
  215.7 17.4 %collective-permute-done = bf16[128,2048]{1,0:T(8,128)(2,1)} collective-permute-done((bf16[128,2048]{1,0:T(8,128)(2,1)}, bf16[128,2048]{1,0:T(8,128)(2,1)}, u32[]{:S(2)}, u32[]{:S(2)}) %collective-permute-start) | collective-permute-done | bytes 524320 | tf_op jit(solution)/shard_map/while/body/eval_jaxpr/ppermute | solution.py:12
  237.0 16.5 %collective-permute-done = bf16[128,2048]{1,0:T(8,128)(2,1)} collective-permute-done((bf16[128,2048]{1,0:T(8,128)(2,1)}, bf16[128,2048]{1,0:T(8,128)(2,1)}, u32[]{:S(2)}, u32[]{:S(2)}) %collective-permute-start) | collective-permute-done | bytes 524320 | tf_op jit(solution)/shard_map/while/body/eval_jaxpr/ppermute | solution.py:12
  257.4 15.7 %collective-permute-done = bf16[128,2048]{1,0:T(8,128)(2,1)} collective-permute-done((bf16[128,2048]{1,0:T(8,128)(2,1)}, bf16[128,2048]{1,0:T(8,128)(2,1)}, u32[]{:S(2)}, u32[]{:S(2)}) %collective-permute-start) | collective-permute-done | bytes 524320 | tf_op jit(solution)/shard_map/while/body/eval_jaxpr/ppermute | solution.py:12
  277.1 14.8 %collective-permute-done = bf16[128,2048]{1,0:T(8,128)(2,1)} collective-permute-done((bf16[128,2048]{1,0:T(8,128)(2,1)}, bf16[128,2048]{1,0:T(8,128)(2,1)}, u32[]{:S(2)}, u32[]{:S(2)}) %collective-permute-start) | collective-permute-done | bytes 524320 | tf_op jit(solution)/shard_map/while/body/eval_jaxpr/ppermute | solution.py:12
  295.8 13.9 %collective-permute-done = bf16[128,2048]{1,0:T(8,128)(2,1)} collective-permute-done((bf16[128,2048]{1,0:T(8,128)(2,1)}, bf16[128,2048]{1,0:T(8,128)(2,1)}, u32[]{:S(2)}, u32[]{:S(2)}) %collective-permute-start) | collective-permute-done | bytes 524320 | tf_op jit(solution)/shard_map/while/body/eval_jaxpr/ppermute | solution.py:12
  313.7 13.1 %collective-permute-done = bf16[128,2048]{1,0:T(8,128)(2,1)} collective-permute-done((bf16[128,2048]{1,0:T(8,128)(2,1)}, bf16[128,2048]{1,0:T(8,128)(2,1)}, u32[]{:S(2)}, u32[]{:S(2)}) %collective-permute-start) | collective-permute-done | bytes 524320 | tf_op jit(solution)/shard_map/while/body/eval_jaxpr/ppermute | solution.py:12
  330.7 13.1 %collective-permute-done = bf16[128,2048]{1,0:T(8,128)(2,1)} collective-permute-done((bf16[128,2048]{1,0:T(8,128)(2,1)}, bf16[128,2048]{1,0:T(8,128)(2,1)}, u32[]{:S(2)}, u32[]{:S(2)}) %collective-permute-start) | collective-permute-done | bytes 524320 | tf_op jit(solution)/shard_map/while/body/eval_jaxpr/ppermute | solution.py:12
  347.8 8.2 %fusion.7 = f32[1536,768]{1,0:T(8,128)S(1)} fusion(bf16[1536,2048]{1,0:T(8,128)(2,1)} %bitcast.40, bf16[1,2048,768]{2,1,0:T(8,128)(2,1)} %param.13), kind=kOutput, calls=%fused_computation.11 | convolution fusion | flops 4831838208 | bytes 14155776 | tf_op jit(solution)/shard_map/dot_general | solution.py:36
  356.0 5.6 multiply_convert_fusion.1
  361.6 5.3 convolution_convert_fusion.1
  367.0 4.8 multiply_convert_fusion
  371.7 224.4 %reduce-scatter.2.cloned.1.call-done = bf16[128,2048]{1,0:T(8,128)(2,1)} async-done(((bf16[2048,2048]{1,0:T(8,128)(2,1)}), bf16[128,2048]{1,0:T(8,128)(2,1)}) %reduce-scatter.2.cloned.1.call-update) | async-done | bytes 524304 | tf_op jit(solution)/shard_map/reduce_scatter | solution.py:79
  (71 shorter events, 63.9 us)
Async XLA Ops:
  6.5 355.1 %copy-start = (bf16[1,768,2048]{2,1,0:T(8,128)(2,1)S(1)}, bf16[1,768,2048]{2,1,0:T(8,128)(2,1)}, u32[]{:S(2)}) copy-start(bf16[1,768,2048]{2,1,0:T(8,128)(2,1)} %param.15) | copy-start | bytes 9437188
  6.5 589.6 %reduce-scatter.2.cloned.1.call-start = ((), (), s32[]{:S(2)}) async-start(), calls=%async_computation.1 | async-start | bytes 8912896 | tf_op jit(solution)/shard_map/reduce_scatter | solution.py:79
  56.1 2.0 copy-start.3
  58.1 2.6 copy-start.1
  60.8 13.1 %collective-permute-start = (bf16[128,2048]{1,0:T(8,128)(2,1)}, bf16[128,2048]{1,0:T(8,128)(2,1)}, u32[]{:S(2)}, u32[]{:S(2)}) collective-permute-start(bf16[128,2048]{1,0:T(8,128)(2,1)} %get-tuple-element.195), channel_id=1, source_target_pairs={{15,0},{0,1},{1,2},{2,3},{3,4},{4,5},{5,6},{6,7},{7,8},{8,9},{9,10... | collective-permute-start | bytes 1572872 | tf_op jit(solution)/shard_map/while/body/eval_jaxpr/ppermute | solution.py:12
  77.8 13.1 %collective-permute-start = (bf16[128,2048]{1,0:T(8,128)(2,1)}, bf16[128,2048]{1,0:T(8,128)(2,1)}, u32[]{:S(2)}, u32[]{:S(2)}) collective-permute-start(bf16[128,2048]{1,0:T(8,128)(2,1)} %get-tuple-element.195), channel_id=1, source_target_pairs={{15,0},{0,1},{1,2},{2,3},{3,4},{4,5},{5,6},{6,7},{7,8},{8,9},{9,10... | collective-permute-start | bytes 1572872 | tf_op jit(solution)/shard_map/while/body/eval_jaxpr/ppermute | solution.py:12
  94.9 13.5 %collective-permute-start = (bf16[128,2048]{1,0:T(8,128)(2,1)}, bf16[128,2048]{1,0:T(8,128)(2,1)}, u32[]{:S(2)}, u32[]{:S(2)}) collective-permute-start(bf16[128,2048]{1,0:T(8,128)(2,1)} %get-tuple-element.195), channel_id=1, source_target_pairs={{15,0},{0,1},{1,2},{2,3},{3,4},{4,5},{5,6},{6,7},{7,8},{8,9},{9,10... | collective-permute-start | bytes 1572872 | tf_op jit(solution)/shard_map/while/body/eval_jaxpr/ppermute | solution.py:12
  112.4 14.7 %collective-permute-start = (bf16[128,2048]{1,0:T(8,128)(2,1)}, bf16[128,2048]{1,0:T(8,128)(2,1)}, u32[]{:S(2)}, u32[]{:S(2)}) collective-permute-start(bf16[128,2048]{1,0:T(8,128)(2,1)} %get-tuple-element.195), channel_id=1, source_target_pairs={{15,0},{0,1},{1,2},{2,3},{3,4},{4,5},{5,6},{6,7},{7,8},{8,9},{9,10... | collective-permute-start | bytes 1572872 | tf_op jit(solution)/shard_map/while/body/eval_jaxpr/ppermute | solution.py:12
  131.0 15.8 %collective-permute-start = (bf16[128,2048]{1,0:T(8,128)(2,1)}, bf16[128,2048]{1,0:T(8,128)(2,1)}, u32[]{:S(2)}, u32[]{:S(2)}) collective-permute-start(bf16[128,2048]{1,0:T(8,128)(2,1)} %get-tuple-element.195), channel_id=1, source_target_pairs={{15,0},{0,1},{1,2},{2,3},{3,4},{4,5},{5,6},{6,7},{7,8},{8,9},{9,10... | collective-permute-start | bytes 1572872 | tf_op jit(solution)/shard_map/while/body/eval_jaxpr/ppermute | solution.py:12
  150.7 17.0 %collective-permute-start = (bf16[128,2048]{1,0:T(8,128)(2,1)}, bf16[128,2048]{1,0:T(8,128)(2,1)}, u32[]{:S(2)}, u32[]{:S(2)}) collective-permute-start(bf16[128,2048]{1,0:T(8,128)(2,1)} %get-tuple-element.195), channel_id=1, source_target_pairs={{15,0},{0,1},{1,2},{2,3},{3,4},{4,5},{5,6},{6,7},{7,8},{8,9},{9,10... | collective-permute-start | bytes 1572872 | tf_op jit(solution)/shard_map/while/body/eval_jaxpr/ppermute | solution.py:12
  171.6 18.1 %collective-permute-start = (bf16[128,2048]{1,0:T(8,128)(2,1)}, bf16[128,2048]{1,0:T(8,128)(2,1)}, u32[]{:S(2)}, u32[]{:S(2)}) collective-permute-start(bf16[128,2048]{1,0:T(8,128)(2,1)} %get-tuple-element.195), channel_id=1, source_target_pairs={{15,0},{0,1},{1,2},{2,3},{3,4},{4,5},{5,6},{6,7},{7,8},{8,9},{9,10... | collective-permute-start | bytes 1572872 | tf_op jit(solution)/shard_map/while/body/eval_jaxpr/ppermute | solution.py:12
  193.6 18.2 %collective-permute-start = (bf16[128,2048]{1,0:T(8,128)(2,1)}, bf16[128,2048]{1,0:T(8,128)(2,1)}, u32[]{:S(2)}, u32[]{:S(2)}) collective-permute-start(bf16[128,2048]{1,0:T(8,128)(2,1)} %get-tuple-element.195), channel_id=1, source_target_pairs={{15,0},{0,1},{1,2},{2,3},{3,4},{4,5},{5,6},{6,7},{7,8},{8,9},{9,10... | collective-permute-start | bytes 1572872 | tf_op jit(solution)/shard_map/while/body/eval_jaxpr/ppermute | solution.py:12
  215.7 17.4 %collective-permute-start = (bf16[128,2048]{1,0:T(8,128)(2,1)}, bf16[128,2048]{1,0:T(8,128)(2,1)}, u32[]{:S(2)}, u32[]{:S(2)}) collective-permute-start(bf16[128,2048]{1,0:T(8,128)(2,1)} %get-tuple-element.195), channel_id=1, source_target_pairs={{15,0},{0,1},{1,2},{2,3},{3,4},{4,5},{5,6},{6,7},{7,8},{8,9},{9,10... | collective-permute-start | bytes 1572872 | tf_op jit(solution)/shard_map/while/body/eval_jaxpr/ppermute | solution.py:12
  237.0 16.5 %collective-permute-start = (bf16[128,2048]{1,0:T(8,128)(2,1)}, bf16[128,2048]{1,0:T(8,128)(2,1)}, u32[]{:S(2)}, u32[]{:S(2)}) collective-permute-start(bf16[128,2048]{1,0:T(8,128)(2,1)} %get-tuple-element.195), channel_id=1, source_target_pairs={{15,0},{0,1},{1,2},{2,3},{3,4},{4,5},{5,6},{6,7},{7,8},{8,9},{9,10... | collective-permute-start | bytes 1572872 | tf_op jit(solution)/shard_map/while/body/eval_jaxpr/ppermute | solution.py:12
  257.4 15.7 %collective-permute-start = (bf16[128,2048]{1,0:T(8,128)(2,1)}, bf16[128,2048]{1,0:T(8,128)(2,1)}, u32[]{:S(2)}, u32[]{:S(2)}) collective-permute-start(bf16[128,2048]{1,0:T(8,128)(2,1)} %get-tuple-element.195), channel_id=1, source_target_pairs={{15,0},{0,1},{1,2},{2,3},{3,4},{4,5},{5,6},{6,7},{7,8},{8,9},{9,10... | collective-permute-start | bytes 1572872 | tf_op jit(solution)/shard_map/while/body/eval_jaxpr/ppermute | solution.py:12
  277.1 14.8 %collective-permute-start = (bf16[128,2048]{1,0:T(8,128)(2,1)}, bf16[128,2048]{1,0:T(8,128)(2,1)}, u32[]{:S(2)}, u32[]{:S(2)}) collective-permute-start(bf16[128,2048]{1,0:T(8,128)(2,1)} %get-tuple-element.195), channel_id=1, source_target_pairs={{15,0},{0,1},{1,2},{2,3},{3,4},{4,5},{5,6},{6,7},{7,8},{8,9},{9,10... | collective-permute-start | bytes 1572872 | tf_op jit(solution)/shard_map/while/body/eval_jaxpr/ppermute | solution.py:12
  295.8 13.9 %collective-permute-start = (bf16[128,2048]{1,0:T(8,128)(2,1)}, bf16[128,2048]{1,0:T(8,128)(2,1)}, u32[]{:S(2)}, u32[]{:S(2)}) collective-permute-start(bf16[128,2048]{1,0:T(8,128)(2,1)} %get-tuple-element.195), channel_id=1, source_target_pairs={{15,0},{0,1},{1,2},{2,3},{3,4},{4,5},{5,6},{6,7},{7,8},{8,9},{9,10... | collective-permute-start | bytes 1572872 | tf_op jit(solution)/shard_map/while/body/eval_jaxpr/ppermute | solution.py:12
  313.7 13.1 %collective-permute-start = (bf16[128,2048]{1,0:T(8,128)(2,1)}, bf16[128,2048]{1,0:T(8,128)(2,1)}, u32[]{:S(2)}, u32[]{:S(2)}) collective-permute-start(bf16[128,2048]{1,0:T(8,128)(2,1)} %get-tuple-element.195), channel_id=1, source_target_pairs={{15,0},{0,1},{1,2},{2,3},{3,4},{4,5},{5,6},{6,7},{7,8},{8,9},{9,10... | collective-permute-start | bytes 1572872 | tf_op jit(solution)/shard_map/while/body/eval_jaxpr/ppermute | solution.py:12
  330.7 13.1 %collective-permute-start = (bf16[128,2048]{1,0:T(8,128)(2,1)}, bf16[128,2048]{1,0:T(8,128)(2,1)}, u32[]{:S(2)}, u32[]{:S(2)}) collective-permute-start(bf16[128,2048]{1,0:T(8,128)(2,1)} %get-tuple-element.195), channel_id=1, source_target_pairs={{15,0},{0,1},{1,2},{2,3},{3,4},{4,5},{5,6},{6,7},{7,8},{8,9},{9,10... | collective-permute-start | bytes 1572872 | tf_op jit(solution)/shard_map/while/body/eval_jaxpr/ppermute | solution.py:12
  347.8 8.2 %copy-start.2 = (bf16[16,96,2048]{2,1,0:T(8,128)(2,1)S(1)}, bf16[16,96,2048]{2,1,0:T(8,128)(2,1)}, u32[]{:S(2)}) copy-start(bf16[16,96,2048]{2,1,0:T(8,128)(2,1)} %get-tuple-element.138) | copy-start | bytes 18874372
  347.8 8.2 %copy-start.6 = (bf16[1,2048,768]{2,1,0:T(8,128)(2,1)S(1)}, bf16[1,2048,768]{2,1,0:T(8,128)(2,1)}, u32[]{:S(2)}) copy-start(bf16[1,2048,768]{2,1,0:T(8,128)(2,1)} %param.14) | copy-start | bytes 9437188
  361.6 5.3 copy-start.4
  361.6 5.3 copy-start.5
Sparse Core Ops, SparseCore 0:
  371.9 224.2 reduce-scatter.1
where the time goes:
time: 605 us; the launch traced here: 603 us
  waiting for transfers between devices  452 us (75%)
  matrix products  55 us (9%)
  blocking collectives  44.7 us (7%)
  local copies, waits for them, and re-layouts  31.7 us (5%)
  between operations  13.5 us (2%)
    ppermute x15, waiting for transfers between devices, passed_along(): return lax.ppermute(block, axis, route)  228 us
    reduce_scatter x1, waiting for transfers between devices, local(): lax.psum_scatter((back * column[:, :, None]).reshape(spanned * local_rows...  224 us
    all_gather x1, blocking collectives, local(): gathered = lax.all_gather(dense, 'expert', axis=0, tiled=True)  44.7 us
    dot_general x16, matrix products, place_block(): jnp.dot(picked, carried, preferred_element_type=jnp.float32)  31.1 us
    while x15, local copies, waits for them, and re-layouts  28.2 us
  transfers between devices with their start and end apart: 16, of which 16 were waited for; matrix products, arithmetic and copies ran while one was open for 0% of the time, Pallas kernels for 0%

commit v1 on v0

--- a/solution.py
+++ b/solution.py
@@ -57,7 +57,9 @@
     down_matrix = w_down[0]
     normed = normalize(tokens, gain)
     dense = gate_dense(expert_ids, gate_values, group)
-    gathered = lax.all_gather(dense, "expert", axis=0, tiled=True)
+    gathered = jnp.concatenate(
+        lax.all_to_all(jnp.stack([dense] * lax.axis_size("expert")), "expert", 0, 0), axis=0
+    )
     column = lax.dynamic_slice_in_dim(gathered, position, 1, 1).reshape(group, local_rows)
     table = dispatch_table(column, capacity)
     buffer = jnp.zeros((group, capacity, width), jnp.bfloat16)

time: 605 us -> 573 us (0.947)
  blocking collectives: 44.7 us -> 0 us
  starting transfers between devices: 0.04 us -> 12 us
    all_gather x1 -> x0, blocking collectives: 44.7 us -> none  [local(): gathered = lax.all_gather(dense, 'expert', axis=0, tiled=True)]
    all_to_all x0 -> x1, starting transfers between devices: none -> 11.2 us  [local(): lax.all_to_all(jnp.stack([dense] * lax.axis_size('expert')), 'expert', 0, 0)]
    all_to_all x0 -> x1, waiting for transfers between devices: none -> 7.23 us  [local(): lax.all_to_all(jnp.stack([dense] * lax.axis_size('expert')), 'expert', 0, 0)]
    ppermute x15, waiting for transfers between devices: 228 us -> 221 us  [passed_along(): return lax.ppermute(block, axis, route)]
  transfers between devices with their start and end apart: 16 -> 17, of which waited for: 16 -> 17; matrix products, arithmetic and copies ran while one was open for 0% -> 1% of each run, Pallas kernels for 0% -> 0%
where the time goes in v1:
time: 573 us; the launch traced here: 571 us
  waiting for transfers between devices  452 us (79%)
  matrix products  55 us (10%)
  local copies, waits for them, and re-layouts  32.3 us (6%)
  between operations  13.5 us (2%)
  starting transfers between devices  12 us (2%)
  other arithmetic  6.54 us (1%)
    reduce_scatter x1, waiting for transfers between devices, local(): lax.psum_scatter((back * column[:, :, None]).reshape(spanned * local_rows...  223 us
    ppermute x15, waiting for transfers between devices, passed_along(): return lax.ppermute(block, axis, route)  221 us
    dot_general x16, matrix products, place_block(): jnp.dot(picked, carried, preferred_element_type=jnp.float32)  31.1 us
    while x15, local copies, waits for them, and re-layouts  28.2 us
  transfers between devices with their start and end apart: 17, of which 17 were waited for; matrix products, arithmetic and copies ran while one was open for 1% of the time, Pallas kernels for 0%

profile of v1, /device:TPU:2, one launch (start us, length us, event | category | flops | bytes accessed | tf_op | source)
XLA Modules:
  0.0 571.0 jit_solution(11115032741991832399)
XLA Ops:
  8.1 11.2 %all-to-all-start = ((f32[16,128,16]{1,2,0:T(8,128)}), f32[16,128,16]{1,2,0:T(8,128)S(1)}, u32[]{:S(2)}, u32[]{:S(2)}) async-start(f32[16,128,16]{1,2,0:T(8,128)} %stack.2), calls=%async_computation | async-start | bytes 262144 | tf_op jit(solution)/shard_map/all_to_all | solution.py:61
  23.2 7.2 %all-to-all-done = f32[16,128,16]{1,2,0:T(8,128)S(1)} async-done(((f32[16,128,16]{1,2,0:T(8,128)}), f32[16,128,16]{1,2,0:T(8,128)S(1)}, u32[]{:S(2)}, u32[]{:S(2)}) %all-to-all-start) | async-done | bytes 131104 | tf_op jit(solution)/shard_map/all_to_all | solution.py:61
  33.4 2.6 copy-done.1
  36.0 281.0 %while.17 = (s32[]{:T(128)}, bf16[16,96,2048]{2,1,0:T(8,128)(2,1)}, bf16[128,2048]{1,0:T(8,128)(2,1)}, s32[]{:T(128)}, bf16[16,96,128]{2,1,0:T(8,128)(2,1)S(1)},...) while((s32[]{:T(128)}, bf16[16,96,2048]{2,1,0:T(8,128)(2,1)}, bf16[128,2048]{1,0:T(8,128)(2,1)}, s32[]{:T(128)}, ...), condition=%wide.region_4.5_spmd, body=%wide.region_3.4_spmd.sunk | while | flops 50528272 | bytes 4089120 | solution.py:74
  36.7 15.4 %collective-permute-done = bf16[128,2048]{1,0:T(8,128)(2,1)} collective-permute-done((bf16[128,2048]{1,0:T(8,128)(2,1)}, bf16[128,2048]{1,0:T(8,128)(2,1)}, u32[]{:S(2)}, u32[]{:S(2)}) %collective-permute-start) | collective-permute-done | bytes 524320 | tf_op jit(solution)/shard_map/while/body/eval_jaxpr/ppermute | solution.py:12
  56.1 15.3 %collective-permute-done = bf16[128,2048]{1,0:T(8,128)(2,1)} collective-permute-done((bf16[128,2048]{1,0:T(8,128)(2,1)}, bf16[128,2048]{1,0:T(8,128)(2,1)}, u32[]{:S(2)}, u32[]{:S(2)}) %collective-permute-start) | collective-permute-done | bytes 524320 | tf_op jit(solution)/shard_map/while/body/eval_jaxpr/ppermute | solution.py:12
  75.4 14.4 %collective-permute-done = bf16[128,2048]{1,0:T(8,128)(2,1)} collective-permute-done((bf16[128,2048]{1,0:T(8,128)(2,1)}, bf16[128,2048]{1,0:T(8,128)(2,1)}, u32[]{:S(2)}, u32[]{:S(2)}) %collective-permute-start) | collective-permute-done | bytes 524320 | tf_op jit(solution)/shard_map/while/body/eval_jaxpr/ppermute | solution.py:12
  93.7 13.6 %collective-permute-done = bf16[128,2048]{1,0:T(8,128)(2,1)} collective-permute-done((bf16[128,2048]{1,0:T(8,128)(2,1)}, bf16[128,2048]{1,0:T(8,128)(2,1)}, u32[]{:S(2)}, u32[]{:S(2)}) %collective-permute-start) | collective-permute-done | bytes 524320 | tf_op jit(solution)/shard_map/while/body/eval_jaxpr/ppermute | solution.py:12
  111.3 13.1 %collective-permute-done = bf16[128,2048]{1,0:T(8,128)(2,1)} collective-permute-done((bf16[128,2048]{1,0:T(8,128)(2,1)}, bf16[128,2048]{1,0:T(8,128)(2,1)}, u32[]{:S(2)}, u32[]{:S(2)}) %collective-permute-start) | collective-permute-done | bytes 524320 | tf_op jit(solution)/shard_map/while/body/eval_jaxpr/ppermute | solution.py:12
  128.3 13.1 %collective-permute-done = bf16[128,2048]{1,0:T(8,128)(2,1)} collective-permute-done((bf16[128,2048]{1,0:T(8,128)(2,1)}, bf16[128,2048]{1,0:T(8,128)(2,1)}, u32[]{:S(2)}, u32[]{:S(2)}) %collective-permute-start) | collective-permute-done | bytes 524320 | tf_op jit(solution)/shard_map/while/body/eval_jaxpr/ppermute | solution.py:12
  145.4 13.1 %collective-permute-done = bf16[128,2048]{1,0:T(8,128)(2,1)} collective-permute-done((bf16[128,2048]{1,0:T(8,128)(2,1)}, bf16[128,2048]{1,0:T(8,128)(2,1)}, u32[]{:S(2)}, u32[]{:S(2)}) %collective-permute-start) | collective-permute-done | bytes 524320 | tf_op jit(solution)/shard_map/while/body/eval_jaxpr/ppermute | solution.py:12
  162.4 13.1 %collective-permute-done = bf16[128,2048]{1,0:T(8,128)(2,1)} collective-permute-done((bf16[128,2048]{1,0:T(8,128)(2,1)}, bf16[128,2048]{1,0:T(8,128)(2,1)}, u32[]{:S(2)}, u32[]{:S(2)}) %collective-permute-start) | collective-permute-done | bytes 524320 | tf_op jit(solution)/shard_map/while/body/eval_jaxpr/ppermute | solution.py:12
  179.4 13.4 %collective-permute-done = bf16[128,2048]{1,0:T(8,128)(2,1)} collective-permute-done((bf16[128,2048]{1,0:T(8,128)(2,1)}, bf16[128,2048]{1,0:T(8,128)(2,1)}, u32[]{:S(2)}, u32[]{:S(2)}) %collective-permute-start) | collective-permute-done | bytes 524320 | tf_op jit(solution)/shard_map/while/body/eval_jaxpr/ppermute | solution.py:12
  196.8 14.6 %collective-permute-done = bf16[128,2048]{1,0:T(8,128)(2,1)} collective-permute-done((bf16[128,2048]{1,0:T(8,128)(2,1)}, bf16[128,2048]{1,0:T(8,128)(2,1)}, u32[]{:S(2)}, u32[]{:S(2)}) %collective-permute-start) | collective-permute-done | bytes 524320 | tf_op jit(solution)/shard_map/while/body/eval_jaxpr/ppermute | solution.py:12
  215.3 15.7 %collective-permute-done = bf16[128,2048]{1,0:T(8,128)(2,1)} collective-permute-done((bf16[128,2048]{1,0:T(8,128)(2,1)}, bf16[128,2048]{1,0:T(8,128)(2,1)}, u32[]{:S(2)}, u32[]{:S(2)}) %collective-permute-start) | collective-permute-done | bytes 524320 | tf_op jit(solution)/shard_map/while/body/eval_jaxpr/ppermute | solution.py:12
  235.0 16.9 %collective-permute-done = bf16[128,2048]{1,0:T(8,128)(2,1)} collective-permute-done((bf16[128,2048]{1,0:T(8,128)(2,1)}, bf16[128,2048]{1,0:T(8,128)(2,1)}, u32[]{:S(2)}, u32[]{:S(2)}) %collective-permute-start) | collective-permute-done | bytes 524320 | tf_op jit(solution)/shard_map/while/body/eval_jaxpr/ppermute | solution.py:12
  255.8 18.0 %collective-permute-done = bf16[128,2048]{1,0:T(8,128)(2,1)} collective-permute-done((bf16[128,2048]{1,0:T(8,128)(2,1)}, bf16[128,2048]{1,0:T(8,128)(2,1)}, u32[]{:S(2)}, u32[]{:S(2)}) %collective-permute-start) | collective-permute-done | bytes 524320 | tf_op jit(solution)/shard_map/while/body/eval_jaxpr/ppermute | solution.py:12
  277.7 18.3 %collective-permute-done = bf16[128,2048]{1,0:T(8,128)(2,1)} collective-permute-done((bf16[128,2048]{1,0:T(8,128)(2,1)}, bf16[128,2048]{1,0:T(8,128)(2,1)}, u32[]{:S(2)}, u32[]{:S(2)}) %collective-permute-start) | collective-permute-done | bytes 524320 | tf_op jit(solution)/shard_map/while/body/eval_jaxpr/ppermute | solution.py:12
  300.0 13.1 %collective-permute-done = bf16[128,2048]{1,0:T(8,128)(2,1)} collective-permute-done((bf16[128,2048]{1,0:T(8,128)(2,1)}, bf16[128,2048]{1,0:T(8,128)(2,1)}, u32[]{:S(2)}, u32[]{:S(2)}) %collective-permute-start) | collective-permute-done | bytes 524320 | tf_op jit(solution)/shard_map/while/body/eval_jaxpr/ppermute | solution.py:12
  317.0 8.2 %fusion.7 = f32[1536,768]{1,0:T(8,128)S(1)} fusion(bf16[1536,2048]{1,0:T(8,128)(2,1)} %bitcast.45, bf16[1,2048,768]{2,1,0:T(8,128)(2,1)} %param.13), kind=kOutput, calls=%fused_computation.11 | convolution fusion | flops 4831838208 | bytes 14155776 | tf_op jit(solution)/shard_map/dot_general | solution.py:36
  325.2 5.6 multiply_convert_fusion.1
  330.9 5.3 convolution_convert_fusion.1
  336.2 4.8 multiply_convert_fusion
  341.0 223.2 %reduce-scatter.2.cloned.1.call-done = bf16[128,2048]{1,0:T(8,128)(2,1)} async-done(((bf16[2048,2048]{1,0:T(8,128)(2,1)}), bf16[128,2048]{1,0:T(8,128)(2,1)}) %reduce-scatter.2.cloned.1.call-update) | async-done | bytes 524304 | tf_op jit(solution)/shard_map/reduce_scatter | solution.py:81
  (74 shorter events, 68.2 us)
Async XLA Ops:
  6.5 324.3 %copy-start = (bf16[1,768,2048]{2,1,0:T(8,128)(2,1)S(1)}, bf16[1,768,2048]{2,1,0:T(8,128)(2,1)}, u32[]{:S(2)}) copy-start(bf16[1,768,2048]{2,1,0:T(8,128)(2,1)} %param.15) | copy-start | bytes 9437188
  8.1 22.3 %all-to-all-start = ((f32[16,128,16]{1,2,0:T(8,128)}), f32[16,128,16]{1,2,0:T(8,128)S(1)}, u32[]{:S(2)}, u32[]{:S(2)}) async-start(f32[16,128,16]{1,2,0:T(8,128)} %stack.2), calls=%async_computation | async-start | bytes 262144 | tf_op jit(solution)/shard_map/all_to_all | solution.py:61
  19.3 544.9 %reduce-scatter.2.cloned.1.call-start = ((), (), s32[]{:S(2)}) async-start(), calls=%async_computation.2 | async-start | bytes 8912896 | tf_op jit(solution)/shard_map/reduce_scatter | solution.py:81
  31.3 1.8 copy-start.3
  33.3 2.7 copy-start.1
  36.0 16.2 %collective-permute-start = (bf16[128,2048]{1,0:T(8,128)(2,1)}, bf16[128,2048]{1,0:T(8,128)(2,1)}, u32[]{:S(2)}, u32[]{:S(2)}) collective-permute-start(bf16[128,2048]{1,0:T(8,128)(2,1)} %get-tuple-element.195), channel_id=1, source_target_pairs={{15,0},{0,1},{1,2},{2,3},{3,4},{4,5},{5,6},{6,7},{7,8},{8,9},{9,10... | collective-permute-start | bytes 1572872 | tf_op jit(solution)/shard_map/while/body/eval_jaxpr/ppermute | solution.py:12
  56.1 15.3 %collective-permute-start = (bf16[128,2048]{1,0:T(8,128)(2,1)}, bf16[128,2048]{1,0:T(8,128)(2,1)}, u32[]{:S(2)}, u32[]{:S(2)}) collective-permute-start(bf16[128,2048]{1,0:T(8,128)(2,1)} %get-tuple-element.195), channel_id=1, source_target_pairs={{15,0},{0,1},{1,2},{2,3},{3,4},{4,5},{5,6},{6,7},{7,8},{8,9},{9,10... | collective-permute-start | bytes 1572872 | tf_op jit(solution)/shard_map/while/body/eval_jaxpr/ppermute | solution.py:12
  75.4 14.4 %collective-permute-start = (bf16[128,2048]{1,0:T(8,128)(2,1)}, bf16[128,2048]{1,0:T(8,128)(2,1)}, u32[]{:S(2)}, u32[]{:S(2)}) collective-permute-start(bf16[128,2048]{1,0:T(8,128)(2,1)} %get-tuple-element.195), channel_id=1, source_target_pairs={{15,0},{0,1},{1,2},{2,3},{3,4},{4,5},{5,6},{6,7},{7,8},{8,9},{9,10... | collective-permute-start | bytes 1572872 | tf_op jit(solution)/shard_map/while/body/eval_jaxpr/ppermute | solution.py:12
  93.7 13.6 %collective-permute-start = (bf16[128,2048]{1,0:T(8,128)(2,1)}, bf16[128,2048]{1,0:T(8,128)(2,1)}, u32[]{:S(2)}, u32[]{:S(2)}) collective-permute-start(bf16[128,2048]{1,0:T(8,128)(2,1)} %get-tuple-element.195), channel_id=1, source_target_pairs={{15,0},{0,1},{1,2},{2,3},{3,4},{4,5},{5,6},{6,7},{7,8},{8,9},{9,10... | collective-permute-start | bytes 1572872 | tf_op jit(solution)/shard_map/while/body/eval_jaxpr/ppermute | solution.py:12
  111.3 13.1 %collective-permute-start = (bf16[128,2048]{1,0:T(8,128)(2,1)}, bf16[128,2048]{1,0:T(8,128)(2,1)}, u32[]{:S(2)}, u32[]{:S(2)}) collective-permute-start(bf16[128,2048]{1,0:T(8,128)(2,1)} %get-tuple-element.195), channel_id=1, source_target_pairs={{15,0},{0,1},{1,2},{2,3},{3,4},{4,5},{5,6},{6,7},{7,8},{8,9},{9,10... | collective-permute-start | bytes 1572872 | tf_op jit(solution)/shard_map/while/body/eval_jaxpr/ppermute | solution.py:12
  128.3 13.1 %collective-permute-start = (bf16[128,2048]{1,0:T(8,128)(2,1)}, bf16[128,2048]{1,0:T(8,128)(2,1)}, u32[]{:S(2)}, u32[]{:S(2)}) collective-permute-start(bf16[128,2048]{1,0:T(8,128)(2,1)} %get-tuple-element.195), channel_id=1, source_target_pairs={{15,0},{0,1},{1,2},{2,3},{3,4},{4,5},{5,6},{6,7},{7,8},{8,9},{9,10... | collective-permute-start | bytes 1572872 | tf_op jit(solution)/shard_map/while/body/eval_jaxpr/ppermute | solution.py:12
  145.4 13.1 %collective-permute-start = (bf16[128,2048]{1,0:T(8,128)(2,1)}, bf16[128,2048]{1,0:T(8,128)(2,1)}, u32[]{:S(2)}, u32[]{:S(2)}) collective-permute-start(bf16[128,2048]{1,0:T(8,128)(2,1)} %get-tuple-element.195), channel_id=1, source_target_pairs={{15,0},{0,1},{1,2},{2,3},{3,4},{4,5},{5,6},{6,7},{7,8},{8,9},{9,10... | collective-permute-start | bytes 1572872 | tf_op jit(solution)/shard_map/while/body/eval_jaxpr/ppermute | solution.py:12
  162.4 13.1 %collective-permute-start = (bf16[128,2048]{1,0:T(8,128)(2,1)}, bf16[128,2048]{1,0:T(8,128)(2,1)}, u32[]{:S(2)}, u32[]{:S(2)}) collective-permute-start(bf16[128,2048]{1,0:T(8,128)(2,1)} %get-tuple-element.195), channel_id=1, source_target_pairs={{15,0},{0,1},{1,2},{2,3},{3,4},{4,5},{5,6},{6,7},{7,8},{8,9},{9,10... | collective-permute-start | bytes 1572872 | tf_op jit(solution)/shard_map/while/body/eval_jaxpr/ppermute | solution.py:12
  179.4 13.4 %collective-permute-start = (bf16[128,2048]{1,0:T(8,128)(2,1)}, bf16[128,2048]{1,0:T(8,128)(2,1)}, u32[]{:S(2)}, u32[]{:S(2)}) collective-permute-start(bf16[128,2048]{1,0:T(8,128)(2,1)} %get-tuple-element.195), channel_id=1, source_target_pairs={{15,0},{0,1},{1,2},{2,3},{3,4},{4,5},{5,6},{6,7},{7,8},{8,9},{9,10... | collective-permute-start | bytes 1572872 | tf_op jit(solution)/shard_map/while/body/eval_jaxpr/ppermute | solution.py:12
  196.8 14.6 %collective-permute-start = (bf16[128,2048]{1,0:T(8,128)(2,1)}, bf16[128,2048]{1,0:T(8,128)(2,1)}, u32[]{:S(2)}, u32[]{:S(2)}) collective-permute-start(bf16[128,2048]{1,0:T(8,128)(2,1)} %get-tuple-element.195), channel_id=1, source_target_pairs={{15,0},{0,1},{1,2},{2,3},{3,4},{4,5},{5,6},{6,7},{7,8},{8,9},{9,10... | collective-permute-start | bytes 1572872 | tf_op jit(solution)/shard_map/while/body/eval_jaxpr/ppermute | solution.py:12
  215.3 15.7 %collective-permute-start = (bf16[128,2048]{1,0:T(8,128)(2,1)}, bf16[128,2048]{1,0:T(8,128)(2,1)}, u32[]{:S(2)}, u32[]{:S(2)}) collective-permute-start(bf16[128,2048]{1,0:T(8,128)(2,1)} %get-tuple-element.195), channel_id=1, source_target_pairs={{15,0},{0,1},{1,2},{2,3},{3,4},{4,5},{5,6},{6,7},{7,8},{8,9},{9,10... | collective-permute-start | bytes 1572872 | tf_op jit(solution)/shard_map/while/body/eval_jaxpr/ppermute | solution.py:12
  235.0 16.9 %collective-permute-start = (bf16[128,2048]{1,0:T(8,128)(2,1)}, bf16[128,2048]{1,0:T(8,128)(2,1)}, u32[]{:S(2)}, u32[]{:S(2)}) collective-permute-start(bf16[128,2048]{1,0:T(8,128)(2,1)} %get-tuple-element.195), channel_id=1, source_target_pairs={{15,0},{0,1},{1,2},{2,3},{3,4},{4,5},{5,6},{6,7},{7,8},{8,9},{9,10... | collective-permute-start | bytes 1572872 | tf_op jit(solution)/shard_map/while/body/eval_jaxpr/ppermute | solution.py:12
  255.8 18.0 %collective-permute-start = (bf16[128,2048]{1,0:T(8,128)(2,1)}, bf16[128,2048]{1,0:T(8,128)(2,1)}, u32[]{:S(2)}, u32[]{:S(2)}) collective-permute-start(bf16[128,2048]{1,0:T(8,128)(2,1)} %get-tuple-element.195), channel_id=1, source_target_pairs={{15,0},{0,1},{1,2},{2,3},{3,4},{4,5},{5,6},{6,7},{7,8},{8,9},{9,10... | collective-permute-start | bytes 1572872 | tf_op jit(solution)/shard_map/while/body/eval_jaxpr/ppermute | solution.py:12
  277.7 18.3 %collective-permute-start = (bf16[128,2048]{1,0:T(8,128)(2,1)}, bf16[128,2048]{1,0:T(8,128)(2,1)}, u32[]{:S(2)}, u32[]{:S(2)}) collective-permute-start(bf16[128,2048]{1,0:T(8,128)(2,1)} %get-tuple-element.195), channel_id=1, source_target_pairs={{15,0},{0,1},{1,2},{2,3},{3,4},{4,5},{5,6},{6,7},{7,8},{8,9},{9,10... | collective-permute-start | bytes 1572872 | tf_op jit(solution)/shard_map/while/body/eval_jaxpr/ppermute | solution.py:12
  300.0 13.1 %collective-permute-start = (bf16[128,2048]{1,0:T(8,128)(2,1)}, bf16[128,2048]{1,0:T(8,128)(2,1)}, u32[]{:S(2)}, u32[]{:S(2)}) collective-permute-start(bf16[128,2048]{1,0:T(8,128)(2,1)} %get-tuple-element.195), channel_id=1, source_target_pairs={{15,0},{0,1},{1,2},{2,3},{3,4},{4,5},{5,6},{6,7},{7,8},{8,9},{9,10... | collective-permute-start | bytes 1572872 | tf_op jit(solution)/shard_map/while/body/eval_jaxpr/ppermute | solution.py:12
  317.0 8.2 %copy-start.2 = (bf16[16,96,2048]{2,1,0:T(8,128)(2,1)S(1)}, bf16[16,96,2048]{2,1,0:T(8,128)(2,1)}, u32[]{:S(2)}) copy-start(bf16[16,96,2048]{2,1,0:T(8,128)(2,1)} %get-tuple-element.138) | copy-start | bytes 18874372
  317.0 8.2 %copy-start.6 = (bf16[1,2048,768]{2,1,0:T(8,128)(2,1)S(1)}, bf16[1,2048,768]{2,1,0:T(8,128)(2,1)}, u32[]{:S(2)}) copy-start(bf16[1,2048,768]{2,1,0:T(8,128)(2,1)} %param.14) | copy-start | bytes 9437188
  330.9 5.3 copy-start.4
  330.9 5.3 copy-start.5
Sparse Core Ops, SparseCore 0:
  341.1 223.0 reduce-scatter.1
